TPU v7x, 32 devices: a whole 2x2x4 slice. The times are simulated.
32 devices in a mesh: vol: 8 (over z, y), orient: 4 (over x, core).
Axes of the slice: x: 2, y: 2, z: 4, core: 2. Of those that a mesh axis runs over, the one named last changes fastest.
Arguments:
- tomogram: bfloat16 [640, 512, 256], P('vol', 'orient'), may hold values from -40 to 40
- templates: bfloat16 [4, 32, 1024], P('orient'), may hold values from 0 to 5
- corner_z: int32 [8, 60], P('vol', 'orient'), may hold values from 0 to 16
- corner_y: int32 [8, 60], P('vol', 'orient'), may hold values from 0 to 64
- corner_x: int32 [8, 60], P('vol', 'orient'), may hold values from 0 to 192
- loads: int32 [8, 4, 8], P('vol', 'orient'), may hold values from 0 to 2, as said below
Outputs:
- peaks: float32 [8, 60, 4], P('vol', 'orient')
- best: float32 [8, 60], P('vol', 'orient')
Inputs may be any that keep to these rules, and one draw needn't show every extreme that they name: `loads`: entry [v, o, m] is the number of candidates that owner (v, o) hands to matcher (m, o). Owner (v, o) holds as many candidates as its row sums to, at most 15, and in every orient column one owner holds exactly 15. Every matcher receives exactly 8 candidates. Some entry equals 2.
All inputs are finite; a program needn't handle non-finite values.
Results may differ from a plain program's by a relative error of at most 0.0064.
Values may be sent and summed in bfloat16 or wider, within the bound.
No kernel may reach another device: no remote copies, remote signals or barrier semaphores. Data moves between devices by JAX's collectives and lax.ppermute only.
A program may use at most 128 MiB of HBM per device.

v0:
```python
import math

import jax
import jax.numpy as jnp
from jax import lax
from jax.sharding import PartitionSpec as P
from jax.experimental import pallas as pl
from jax.experimental.pallas import tpu as pltpu

BOX = 64
TMPL = 32
SHIFT = 8
HALF = 33


epsilon = 1e-05


def shift_anchor():
    return (BOX - TMPL) // 2 - SHIFT // 2


def angle_of(turn_index):
    return turn_index.astype(jnp.float32) * (2.0 * math.pi / BOX)


def phases(count_out, count_in, offset):
    out_index = jnp.arange(count_out, dtype=jnp.int32) + offset
    in_index = jnp.arange(count_in, dtype=jnp.int32)
    turn_index = out_index[:, None] * in_index[None, :] % BOX
    phase_angle = angle_of(turn_index)
    return (jnp.cos(phase_angle), jnp.sin(phase_angle))


def bf(x):
    return x.astype(jnp.bfloat16)


def complex_table(cos_t, sin_t, sign_re_from_im, sign_im_from_re):
    c = bf(cos_t).T
    s = bf(sin_t).T
    re_row = jnp.stack([c, sign_im_from_re * s], axis=1)
    im_row = jnp.stack([sign_re_from_im * s, c], axis=1)
    return jnp.stack([re_row, im_row], axis=0)


def section(pattern, operand, table):
    return jnp.einsum(pattern, bf(operand), table, preferred_element_type=jnp.float32)


def forward_tail(stage_one):
    length_a = stage_one.shape[2]
    length_y = stage_one.shape[3]
    cos_full, sin_full = phases(BOX, length_y, 0)
    t_mid = complex_table(cos_full, sin_full, 1.0, -1.0)
    stage_two = section("ncayk,cydj->ndajk", stage_one, t_mid)
    cos_half, sin_half = phases(HALF, length_a, 0)
    t_first = complex_table(cos_half, sin_half, 1.0, -1.0)
    return section("ncajk,cadh->ndhjk", stage_two, t_first)


def template_spectra(cubes):
    volume = cubes.astype(jnp.float32)
    count = volume.shape[0]
    flat = volume.reshape(count, -1)
    centred = flat - jnp.mean(flat, axis=1, keepdims=True)
    unit = centred / jnp.sqrt(jnp.mean(centred * centred, axis=1, keepdims=True) + epsilon)
    cos_full, sin_full = phases(BOX, TMPL, 0)
    c_full = bf(cos_full).T
    s_full = bf(sin_full).T
    t_last = jnp.concatenate([c_full, -s_full], axis=1)
    stage_one = jnp.dot(bf(unit).reshape(count * TMPL * TMPL, TMPL), t_last, preferred_element_type=jnp.float32)
    stage_one = bf(stage_one).reshape(count, TMPL, TMPL, 2, BOX)
    stacked = jnp.transpose(stage_one, (0, 1, 4, 3, 2)).reshape(count * TMPL * BOX, 2 * TMPL)
    t_mid = jnp.concatenate(
        [jnp.concatenate([c_full, -s_full], axis=1), jnp.concatenate([s_full, c_full], axis=1)], axis=0
    )
    stage_two = jnp.dot(stacked, t_mid, preferred_element_type=jnp.float32)
    stage_two = bf(stage_two).reshape(count, TMPL, BOX, 2 * BOX)
    swapped = jnp.concatenate([stage_two[..., BOX:], -stage_two[..., :BOX]], axis=-1)
    pair = jnp.stack([stage_two, swapped], axis=1)
    cos_half, sin_half = phases(HALF, TMPL, 0)
    t_first = jnp.stack([bf(cos_half).T, bf(sin_half).T], axis=0)
    return bf(jnp.einsum("rwakq,wah->rhkq", pair, t_first, preferred_element_type=jnp.float32))


def window_table(corner_x, width):
    pos = jnp.arange(width, dtype=jnp.int32)[None, :] - corner_x[:, None]
    inside = (pos >= 0) & (pos < BOX)
    k = jnp.arange(BOX, dtype=jnp.int32)
    turn = k[None, None, :] * pos[:, :, None] % BOX
    phase_angle = angle_of(turn)
    mask = inside[:, :, None]
    cos_t = jnp.where(mask, bf(jnp.cos(phase_angle)), jnp.zeros((), jnp.bfloat16))
    sin_t = jnp.where(mask, -bf(jnp.sin(phase_angle)), jnp.zeros((), jnp.bfloat16))
    return jnp.stack([cos_t, sin_t], axis=2)


def band_table():
    lower_edge = jnp.arange(SHIFT, dtype=jnp.int32)[:, None] + shift_anchor()
    cell_index = jnp.arange(BOX, dtype=jnp.int32)[None, :]
    return ((cell_index >= lower_edge) & (cell_index < lower_edge + TMPL)).astype(jnp.float32)


def window_band(corner_x, width):
    lower_edge = jnp.arange(SHIFT, dtype=jnp.int32)[None, :, None] + shift_anchor() + corner_x[:, None, None]
    cell_index = jnp.arange(width, dtype=jnp.int32)[None, None, :]
    return ((cell_index >= lower_edge) & (cell_index < lower_edge + TMPL)).astype(jnp.float32)


def window_rms(rows, corner_x):
    width = rows.shape[-1]
    squares = rows.astype(jnp.float32) ** 2
    band_x = window_band(corner_x, width)
    band = band_table()
    hi = lax.Precision.HIGHEST
    sums_c = jnp.einsum("nabx,nux->nabu", squares, band_x, precision=hi)
    sums_b = jnp.einsum("nabu,tb->natu", sums_c, band, precision=hi)
    sums_a = jnp.einsum("natu,sa->nstu", sums_b, band, precision=hi)
    return jnp.sqrt(sums_a / float(TMPL**3) + epsilon)


def match(box_spectra, box_rms, spectra):
    values = lax.map(lambda one: match_one(box_spectra, box_rms, one[None]), spectra)
    return values[:, :, 0].T


def match_one(box_spectra, box_rms, spectra):
    real_t = spectra[:, 0].astype(jnp.float32)[None]
    imag_t = spectra[:, 1].astype(jnp.float32)[None]
    real_v = box_spectra[:, 0][:, None]
    imag_v = box_spectra[:, 1][:, None]
    real_p = real_t * real_v + imag_t * imag_v
    imag_p = real_t * imag_v - imag_t * real_v
    cross = jnp.stack([bf(real_p), bf(imag_p)], axis=2)
    cos_first, sin_first = phases(SHIFT, HALF, shift_anchor())
    freq_index = jnp.arange(HALF, dtype=jnp.int32)
    weight = jnp.where(freq_index % (BOX // 2) == 0, 1.0, 2.0) / float(BOX**3)
    cos_first = cos_first * weight[None, :]
    sin_first = sin_first * weight[None, :]
    t_first = complex_table(cos_first, sin_first, -1.0, 1.0)
    stage_g = section("nrchjk,chds->nrdsjk", cross, t_first)
    cos_rest, sin_rest = phases(SHIFT, BOX, shift_anchor())
    t_mid = complex_table(cos_rest, sin_rest, -1.0, 1.0)
    stage_h = section("nrcsjk,cjdt->nrdstk", stage_g, t_mid)
    t_last = jnp.stack([bf(cos_rest).T, -bf(sin_rest).T], axis=0)
    correlation = section("nrcstk,cku->nrstu", stage_h, t_last)
    scores = correlation / (box_rms[:, None] * math.sqrt(float(TMPL**3)))
    return jnp.max(scores, axis=(2, 3, 4))


def front_kernel(cz_ref, ys_ref, slab_ref, t1_ref, l2_ref, q2_ref):
    depth, window_y, width = slab_ref.shape
    rows_y = 2 * BOX
    chunk = 8
    t1 = t1_ref[...]
    l2 = l2_ref[...]

    def transform_chunk(ci, carry):
        z0 = pl.multiple_of(ci * chunk, chunk)
        rows = slab_ref[pl.ds(z0, chunk)].reshape(chunk * window_y, width)
        p1 = jnp.dot(rows, t1, preferred_element_type=jnp.float32)
        p1 = p1.astype(jnp.bfloat16).astype(jnp.float32).reshape(chunk, window_y, 2 * BOX)
        pad = jnp.zeros((chunk, rows_y - window_y, 2 * BOX), jnp.float32)
        p1 = jnp.concatenate([p1, pad], axis=1)
        p1t = jnp.swapaxes(p1, 1, 2)
        stacked = jnp.concatenate([p1t[:, :BOX], p1t[:, BOX:]], axis=2)
        stacked = stacked.reshape(chunk * BOX, 2 * rows_y).astype(jnp.bfloat16)
        m2 = jnp.dot(stacked, l2, preferred_element_type=jnp.float32).reshape(chunk, BOX, 2 * BOX)
        lane = lax.broadcasted_iota(jnp.int32, m2.shape, 2)
        sign = jnp.where(lane < BOX, 1.0, -1.0).astype(jnp.float32)
        out = m2.astype(jnp.bfloat16).astype(jnp.float32)
        q2_ref[0, pl.ds(z0, chunk)] = out.astype(jnp.bfloat16)
        swapped = sign * pltpu.roll(out, BOX, 2)
        q2_ref[1, pl.ds(z0, chunk)] = swapped.astype(jnp.bfloat16)
        return carry

    lax.fori_loop(0, depth // chunk, transform_chunk, 0)


def window_bands(corner, length):
    lower_edge = jnp.arange(SHIFT, dtype=jnp.int32)[None, :, None] + shift_anchor() + corner[:, None, None]
    cell_index = jnp.arange(length, dtype=jnp.int32)[None, None, :]
    return ((cell_index >= lower_edge) & (cell_index < lower_edge + TMPL)).astype(jnp.float32)


def block_rms(tomogram, corner_z, corner_y, corner_x):
    depth, rows_y, width = tomogram.shape
    count = corner_z.shape[0]
    hi = lax.Precision.HIGHEST
    values = tomogram.astype(jnp.float32)
    squares = (values * values).reshape(depth * rows_y, width)
    square_hi = bf(squares)
    square_lo = bf(squares - square_hi.astype(jnp.float32))
    band_x = bf(window_bands(corner_x, width).reshape(count * SHIFT, width).T)
    sums_x = jnp.dot(square_hi, band_x, preferred_element_type=jnp.float32)
    sums_x = sums_x + jnp.dot(square_lo, band_x, preferred_element_type=jnp.float32)
    sums_x = sums_x.reshape(depth, rows_y, count, SHIFT)
    band_y = window_bands(corner_y, rows_y)
    sums_y = jnp.einsum("zynu,nty->nztu", sums_x, band_y, precision=hi)
    band_z = window_bands(corner_z, depth)
    sums_z = jnp.einsum("nztu,nsz->nstu", sums_y, band_z, precision=hi)
    return jnp.sqrt(sums_z / float(TMPL**3) + epsilon)


def front(tomogram, corner_z, corner_y, corner_x):
    count = corner_z.shape[0]
    block_y = tomogram.shape[1]
    window_y = BOX + 16
    rows_y = 2 * BOX
    width = tomogram.shape[2]
    start_y = jnp.minimum((corner_y // 16) * 16, block_y - window_y).astype(jnp.int32)
    t1 = window_table(corner_x, width).reshape(count, width, 2 * BOX)
    pos_y = jnp.arange(rows_y, dtype=jnp.int32)[None, :] - (corner_y - start_y)[:, None]
    inside_y = (pos_y >= 0) & (pos_y < BOX)
    j = jnp.arange(BOX, dtype=jnp.int32)
    turn_y = pos_y[:, :, None] * j[None, None, :] % BOX
    angle_y = angle_of(turn_y)
    zero = jnp.zeros((), jnp.bfloat16)
    cos_y = jnp.where(inside_y[:, :, None], bf(jnp.cos(angle_y)), zero)
    sin_y = jnp.where(inside_y[:, :, None], bf(jnp.sin(angle_y)), zero)
    l2 = jnp.concatenate(
        [jnp.concatenate([cos_y, -sin_y], axis=2), jnp.concatenate([sin_y, cos_y], axis=2)], axis=1
    )

    grid_spec = pltpu.PrefetchScalarGridSpec(
        num_scalar_prefetch=2,
        grid=(count,),
        in_specs=[
            pl.BlockSpec(
                (pl.Element(BOX), pl.Element(window_y), pl.Element(width)), lambda n, cz, ys: (cz[n], pl.multiple_of(ys[n], 16), 0)
            ),
            pl.BlockSpec((None, width, 2 * BOX), lambda n, cz, ys: (n, 0, 0)),
            pl.BlockSpec((None, 2 * rows_y, 2 * BOX), lambda n, cz, ys: (n, 0, 0)),
        ],
        out_specs=pl.BlockSpec((None, 2, BOX, BOX, 2 * BOX), lambda n, cz, ys: (n, 0, 0, 0, 0)),
    )
    q2 = pl.pallas_call(
        front_kernel,
        grid_spec=grid_spec,
        out_shape=jax.ShapeDtypeStruct((count, 2, BOX, BOX, 2 * BOX), jnp.bfloat16),
        compiler_params=pltpu.CompilerParams(vmem_limit_bytes=48 * 1024 * 1024),
    )(corner_z, start_y, tomogram, t1, l2)
    return q2, block_rms(tomogram, corner_z, corner_y, corner_x)


def box_spectra_of(q2):
    cos_half, sin_half = phases(HALF, BOX, 0)
    l3 = jnp.stack([bf(cos_half).T, bf(sin_half).T], axis=0)
    return bf(jnp.einsum("nwzkq,wzh->nhkq", q2, l3, preferred_element_type=jnp.float32))


def match_kj(spectrum_v, box_rms, spectra):
    spectra_kj = spectra

    def one(spectrum):
        real_v = spectrum_v[..., :BOX]
        imag_v = spectrum_v[..., BOX:]
        real_t = spectrum[..., :BOX].astype(jnp.float32)[None, None]
        imag_t = spectrum[..., BOX:].astype(jnp.float32)[None, None]
        rv = real_v[:, None]
        iv = imag_v[:, None]
        real_p = real_t * rv + imag_t * iv
        imag_p = real_t * iv - imag_t * rv
        cross = jnp.stack([bf(real_p), bf(imag_p)], axis=2)
        cos_first, sin_first = phases(SHIFT, HALF, shift_anchor())
        freq_index = jnp.arange(HALF, dtype=jnp.int32)
        weight = jnp.where(freq_index % (BOX // 2) == 0, 1.0, 2.0) / float(BOX**3)
        t_first = complex_table(cos_first * weight[None, :], sin_first * weight[None, :], -1.0, 1.0)
        stage_g = section("nrchkj,chds->nrdskj", cross, t_first)
        cos_rest, sin_rest = phases(SHIFT, BOX, shift_anchor())
        t_mid = complex_table(cos_rest, sin_rest, -1.0, 1.0)
        stage_h = section("nrcskj,cjdt->nrdskt", stage_g, t_mid)
        t_last = jnp.stack([bf(cos_rest).T, -bf(sin_rest).T], axis=0)
        correlation = section("nrcskt,cku->nrstu", stage_h, t_last)
        scores = correlation / (box_rms[:, None] * math.sqrt(float(TMPL**3)))
        return jnp.max(scores, axis=(2, 3, 4))[:, 0]

    count_r = spectra_kj.shape[0]
    group = min(4, count_r)

    def one_group(block):
        return jnp.stack([one(block[i]) for i in range(group)], axis=0)

    blocks = spectra_kj.reshape((count_r // group, group) + spectra_kj.shape[1:])
    if count_r == group:
        values = one_group(blocks[0])
    else:
        values = lax.map(one_group, blocks).reshape((count_r,) + (spectrum_v.shape[0],))
    return values.T


def per_device(tomogram, templates, corner_z, corner_y, corner_x, loads):
    own_total = corner_z.shape[1]
    live_count = jnp.sum(loads[0, 0])
    q2, box_rms = front(tomogram, corner_z[0], corner_y[0], corner_x[0])
    spectrum_v = box_spectra_of(q2)

    own_spectra = template_spectra(templates.reshape(-1, TMPL, TMPL, TMPL))
    spectra = lax.all_gather(own_spectra, "orient", axis=0, tiled=True)
    values = match_kj(spectrum_v, box_rms, spectra)
    live = jnp.arange(own_total, dtype=jnp.int32) < live_count
    matched = jnp.where(live[:, None], values, 0.0)
    return (matched[None], jnp.max(matched, axis=1)[None])


def solution(mesh):
    return jax.shard_map(
        per_device,
        mesh=mesh,
        in_specs=(
            P("vol", "orient", None),
            P("orient", None, None),
            P("vol", "orient"),
            P("vol", "orient"),
            P("vol", "orient"),
            P("vol", "orient", None),
        ),
        out_specs=(P("vol", "orient", None), P("vol", "orient")),
        check_vma=False,
    )
```

profile of v0, /device:TPU:0, one launch (start us, length us, event | category | flops | bytes accessed | tf_op | source)
XLA Modules:
  0.0 260.4 jit_solution(6223125816196193759)
XLA Ops:
  7.5 1.5 convert_reduce_fusion
  9.6 1.5 fusion.144
  11.8 0.9 fusion.145
  13.8 0.5 reshape.1177
  14.2 0.4 convolution_convert_fusion
  14.6 0.3 copy.53
  15.5 0.4 copy_negate_fusion
  16.2 0.4 fusion.69
  16.6 1.0 copy.54
  17.9 0.6 reduce_sum.27
  18.5 0.6 iota_compare_fusion.8
  19.6 4.4 %fusion.135 = (bf16[15,256,1,64]{1,3,2,0:T(8,128)(2,1)S(1)}, bf16[15,256,1,64]{1,3,2,0:T(8,128)(2,1)S(1)}) fusion(s32[15,256]{1,0:T(8,128)S(1)} %iota_subtract_fusion, pred[15,256]{1,0:T(8,128)(4,1)S(1)} %compare_and_fusion), kind=kLoop, calls=%fused_computation.159 | loop fusion | flops 5160960 | bytes 1002240 | tf_op jit(solution)/shard_map/jit(_where)/select_n | solution.py:94
  24.1 0.8 copy.56.t1_ref
  24.9 4.2 %convert_multiply_fusion.16 = f32[80,128,256]{2,1,0:T(8,128)S(1)} fusion(bf16[80,128,256]{2,1,0:T(8,128)(2,1)} %slab_ref.1), kind=kLoop, calls=%fused_computation.55 | loop fusion | flops 5242880 | bytes 15728640 | tf_op jit(solution)/shard_map/mul | solution.py:192
  29.2 1.4 fusion.30
  30.7 1.8 fusion.147
  32.5 1.8 fusion.68
  34.3 5.1 %fusion.106 = f32[15,80,8,8]{1,2,3,0:T(8,128)S(1)} fusion(f32[80,128,15,8]{1,3,0,2:T(8,128)S(1)} %fusion.68, s32[15,8]{1,0:T(8,128)S(1)} %get-tuple-element.47, s32[15,8]{1,0:T(8,128)S(1)} %get-tuple-element.48), kind=kOutput, calls=%fused_computation.109 | convolution fusion | flops 118010880 | bytes 5223360 | tf_op jit(solution)/shard_map/zynu,nty->nztu/dot_general | solution.py:200
  39.4 3.4 %fusion.140 = f32[15,8,8,8]{3,1,2,0:T(8,128)S(1)} fusion(f32[15,80,8,8]{1,2,3,0:T(8,128)S(1)} %fusion.106, s32[15,8]{1,0:T(8,128)S(1)} %get-tuple-element.42, s32[15,8]{1,0:T(8,128)S(1)} %get-tuple-element.41), kind=kOutput, calls=%fused_computation.164 | convolution fusion | flops 7401600 | bytes 338880 | tf_op jit(solution)/shard_map/nztu,nsz->nstu/dot_general | solution.py:202
  42.8 0.5 copy.64
  43.3 4.8 %fusion.148 = (bf16[15,128,64]{2,1,0:T(8,128)(2,1)S(1)}, bf16[15,128,64]{2,1,0:T(8,128)(2,1)S(1)}, bf16[15,128,64]{2,1,0:T(8,128)(2,1)S(1)}) fusion(s32[15,128]{1,0:T(8,128)S(1)} %iota_subtract_fusion.1, pred[15,128]{1,0:T(8,128)(4,1)S(1)} %compare_and_fusion.1), kind=kLoop, calls=%fused_computation.178 | loop fusion | flops 2580480 | bytes 746880 | tf_op jit(solution)/shard_map/neg | solution.py:223
  48.1 0.5 maximum_maximum_fusion.l2_ref
  48.6 75.6 %shard_map.77 = bf16[15,2,64,64,128]{4,3,2,1,0:T(8,128)(2,1)} custom-call(s32[15]{0:T(128)S(1)} %bitcast.325, s32[15]{0:T(128)S(1)} %get-tuple-element.7.ys_ref, bf16[80,128,256]{2,1,0:T(8,128)(2,1)} %slab_ref.1, bf16[15,256,128]{2,1,0:T(8,128)(2,1)S(1)} %copy.56.t1_ref, bf16[15,256,128]{2,1,0:T(8,128)(2,1)S(1)} %maximum_maximum_fusion.l2_ref), custom_call_target="tpu_custom_call" | custom-call | tf_op jit(solution)/shard_map/pallas_call | solution.py:238
  125.0 32.5 %fusion.31 = bf16[15,33,64,128]{3,1,2,0:T(8,128)(2,1)} fusion(bf16[15,2,64,64,128]{4,3,2,1,0:T(8,128)(2,1)} %shard_map.77, bf16[1,64,33]{1,2,0:T(8,128)(2,1)S(1)} %get-tuple-element.55, bf16[1,64,33]{1,2,0:T(8,128)(2,1)S(1)} %get-tuple-element.56), kind=kOutput, calls=%fused_computation.56 | convolution fusion | flops 1042162176 | bytes 39575808 | tf_op jit(solution)/shard_map/nwzkq,wzh->nhkq/dot_general | solution.py:250
  157.5 3.6 %slice_convert_fusion.7 = (f32[33,64,64]{2,1,0:T(8,128)S(1)}, f32[33,64,64]{2,1,0:T(8,128)S(1)}, f32[33,64,64]{2,1,0:T(8,128)S(1)}, f32[33,64,64]{2,1,0:T(8,128)...) fusion(bf16[132,64,128]{2,1,0:T(8,128)(2,1)} %all-gather.3.clon, ...), kind=kLoop, calls=%fused_computation.151 | loop fusion | flops 1081344 | bytes 6488064 | tf_op jit(solution)/shard_map/convert_element_type | solution.py:259
  161.1 0.6 copy.55
  161.7 0.6 copy.76
  162.4 0.6 copy.71
  163.0 0.6 copy.70
  163.7 0.6 copy.66
  164.3 0.6 copy.65
  165.0 1.7 copy.58
  166.7 1.7 copy.75
  168.4 11.0 %fusion.37 = (bf16[15,1,1,33,64,64]{5,3,4,0,2,1:T(8,128)(2,1)}, bf16[15,1,1,33,64,64]{5,3,4,0,2,1:T(8,128)(2,1)}) fusion(f32[33,64,64]{2,0,1:T(8,128)S(1)} %copy.66, f32[33,64,64]{2,0,1:T(8,128)S(1)} %copy.65, bf16[15,33,64,128]{3,1,2,0:T(8,128)(2,1)S(1)} %bitcast.327), kind=kLoop, calls=%fused_computation.62 | loop fusion | flops 20275200 | bytes 17301504 | tf_op jit(solution)/shard_map/stack | solution.py:265
  179.4 9.9 %fusion.45 = bf16[15,2,8,64,64]{4,2,3,0,1:T(8,128)(2,1)} fusion(bf16[1,33,2,8]{1,3,0,2:T(8,128)(2,1)S(1)} %get-tuple-element.40, bf16[1,33,2,8]{1,3,0,2:T(8,128)(2,1)S(1)} %get-tuple-element.39, bf16[15,1,1,33,64,64]{5,3,4,0,2,1:T(8,128)(2,1)} %get-tuple-element.11, bf16[15,1,1,33,64,64]{5,3,4,0,2,1:T(8,128)(2,1)} %get-tuple-element.10), kind=kOutput, calls=%fused_computation.72 | convolution fusion | flops 134803584 | bytes 10078272 | tf_op jit(solution)/shard_map/nrchkj,chds->nrdskj/dot_general | solution.py:48
  189.3 27.6 %fusion.39 = (bf16[15,1,1,33,64,64]{5,3,4,0,2,1:T(8,128)(2,1)}, bf16[15,1,1,33,64,64]{5,3,4,0,2,1:T(8,128)(2,1)}, bf16[15,1,1,33,64,64]{5,3,4,0,2,1:T(8,128)(2,1...) fusion(f32[33,64,64]{2,0,1:T(8,128)} %copy.58, ...), kind=kLoop, calls=%fused_computation.64 | loop fusion | flops 52715520 | bytes 35684352 | tf_op jit(solution)/shard_map/stack | solution.py:265
  216.9 8.8 %fusion.44 = bf16[15,2,8,64,64]{4,2,3,0,1:T(8,128)(2,1)S(1)} fusion(bf16[1,33,2,8]{1,3,0,2:T(8,128)(2,1)S(1)} %get-tuple-element.40, bf16[1,33,2,8]{1,3,0,2:T(8,128)(2,1)S(1)} %get-tuple-element.39, bf16[15,1,1,33,64,64]{5,3,4,0,2,1:T(8,128)(2,1)} %get-tuple-element.9, bf16[15,1,1,33,64,64]{5,3,4,0,2,1:T(8,128)(2,1)} %get-tuple-element.8), kind=kOutput, calls=%fused_computation.71 | convolution fusion | flops 134803584 | bytes 10078272 | tf_op jit(solution)/shard_map/nrchkj,chds->nrdskj/dot_general | solution.py:48
  225.7 1.6 fusion.97
  227.3 1.6 fusion.94
  228.9 0.8 fusion.112
  229.7 0.8 fusion.110
  230.5 9.0 %fusion.46 = bf16[15,2,8,64,64]{4,2,3,0,1:T(8,128)(2,1)S(1)} fusion(bf16[1,33,2,8]{1,3,0,2:T(8,128)(2,1)S(1)} %get-tuple-element.40, bf16[1,33,2,8]{1,3,0,2:T(8,128)(2,1)S(1)} %get-tuple-element.39, bf16[15,1,1,33,64,64]{5,3,4,0,2,1:T(8,128)(2,1)} %get-tuple-element.18, bf16[15,1,1,33,64,64]{5,3,4,0,2,1:T(8,128)(2,1)} %get-tuple-element.19), kind=kOutput, calls=%fused_computation.73 | convolution fusion | flops 134803584 | bytes 10078272 | tf_op jit(solution)/shard_map/nrchkj,chds->nrdskj/dot_general | solution.py:48
  239.5 1.6 fusion.100
  241.2 7.8 %fusion.47 = bf16[15,2,8,64,64]{4,2,3,0,1:T(8,128)(2,1)S(1)} fusion(bf16[1,33,2,8]{1,3,0,2:T(8,128)(2,1)S(1)} %get-tuple-element.40, bf16[1,33,2,8]{1,3,0,2:T(8,128)(2,1)S(1)} %get-tuple-element.39, bf16[15,1,1,33,64,64]{5,3,4,0,2,1:T(8,128)(2,1)S(1)} %bitcast.329, bf16[15,1,1,33,64,64]{5,3,4,0,2,1:T(8,128)(2,1)} %get-tuple-element.17), kind=kOutput, calls=%fused_computation.74 | convolution fusion | flops 134803584 | bytes 10078272 | tf_op jit(solution)/shard_map/nrchkj,chds->nrdskj/dot_general | solution.py:48
  249.0 1.6 fusion.103
  250.6 0.8 fusion.116
  251.4 0.8 fusion.114
  252.2 1.1 fusion.220
  (60 shorter events, 3.9 us)
Async XLA Ops:
  7.2 10.4 %copy-start.3 = (s32[1,15]{1,0:T(1,128)S(1)}, s32[1,15]{1,0:T(1,128)}, u32[]{:S(2)}) copy-start(s32[1,15]{1,0:T(1,128)} %param.9) | copy-start | bytes 184
  7.2 10.6 %copy-start.2 = (s32[1,15]{1,0:T(1,128)S(1)}, s32[1,15]{1,0:T(1,128)}, u32[]{:S(2)}) copy-start(s32[1,15]{1,0:T(1,128)} %param.10) | copy-start | bytes 184
  7.2 10.7 %copy-start.4 = (s32[1,1,8]{2,1,0:T(1,128)S(1)}, s32[1,1,8]{2,1,0:T(1,128)}, u32[]{:S(2)}) copy-start(s32[1,1,8]{2,1,0:T(1,128)} %param.11) | copy-start | bytes 100
  7.2 150.3 %all-gather.3.cloned.1.call-start = ((), (), s32[]{:S(2)}) async-start(), calls=%async_computation | async-start | bytes 2703360 | tf_op jit(solution)/shard_map/all_gather | solution.py:300
  29.1 1.5 copy-start
  157.5 10.9 %slice-start = ((s8[9830400]{0:T(1024)(128)(4,1)}), s8[4194304]{0:T(1024)(128)(4,1)S(1)}, s32[]{:S(2)}) async-start(s8[9830400]{0:T(1024)(128)(4,1)} %bitcast.326), calls=%async_computation.1 | async-start | bytes 8388608
  157.5 10.9 %slice-start.1 = ((s8[9830400]{0:T(1024)(128)(4,1)}), s8[4194304]{0:T(1024)(128)(4,1)S(1)}, s32[]{:S(2)}) async-start(s8[9830400]{0:T(1024)(128)(4,1)} %bitcast.326), calls=%async_computation.2 | async-start | bytes 8388608
  163.0 5.4 %slice-start.2 = ((s8[9830400]{0:T(1024)(128)(4,1)}), s8[1441792]{0:T(1024)(128)(4,1)S(1)}, s32[]{:S(2)}) async-start(s8[9830400]{0:T(1024)(128)(4,1)} %bitcast.326), calls=%async_computation.3 | async-start | bytes 2883584
  216.9 8.8 %copy-start.1 = (bf16[15,2,8,64,64]{4,2,3,0,1:T(8,128)(2,1)S(1)}, bf16[15,2,8,64,64]{4,2,3,0,1:T(8,128)(2,1)}, u32[]{:S(2)}) copy-start(bf16[15,2,8,64,64]{4,2,3,0,1:T(8,128)(2,1)} %fusion.45) | copy-start | bytes 5898244
  229.7 11.4 %slice-start.3 = ((s8[9830400]{0:T(1024)(128)(4,1)}), s8[4194304]{0:T(1024)(128)(4,1)S(1)}, s32[]{:S(2)}) async-start(s8[9830400]{0:T(1024)(128)(4,1)} %bitcast.328), calls=%async_computation.4 | async-start | bytes 8388608
  230.5 10.6 %slice-start.4 = ((s8[9830400]{0:T(1024)(128)(4,1)}), s8[4194304]{0:T(1024)(128)(4,1)S(1)}, s32[]{:S(2)}) async-start(s8[9830400]{0:T(1024)(128)(4,1)} %bitcast.328), calls=%async_computation.5 | async-start | bytes 8388608
  230.5 10.7 %slice-start.5 = ((s8[9830400]{0:T(1024)(128)(4,1)}), s8[1441792]{0:T(1024)(128)(4,1)S(1)}, s32[]{:S(2)}) async-start(s8[9830400]{0:T(1024)(128)(4,1)} %bitcast.328), calls=%async_computation.6 | async-start | bytes 2883584
Sparse Core Ops, SparseCore 0:
  17.7 25.6 all-gather.2
where the time goes:
time: 265 us; the launch traced here: 260 us
  matrix products  90.6 us (34%)
  Pallas kernels  75.6 us (29%)
  other arithmetic  66 us (25%)
  between operations  16.1 us (6%)
  local copies, waits for them, and re-layouts  12 us (5%)
    pallas_call x1, Pallas kernels, front(): pl.pallas_call(front_kernel, grid_spec=grid_spec, out_shape=jax.ShapeDtyp...  75.6 us
    dot_general x12, matrix products, section(): jnp.einsum(pattern, bf(operand), table, preferred_element_type=jnp.float32)  45.1 us
    another operation x2, other arithmetic, one(): cross = jnp.stack([bf(real_p), bf(imag_p)], axis=2)  38.6 us
    dot_general x1, matrix products, box_spectra_of(): jnp.einsum('nwzkq,wzh->nhkq', q2, l3, preferred_element_type=jnp.float32)  32.5 us
  transfers between devices with their start and end apart: 1, of which 0 were waited for; matrix products, arithmetic and copies ran while one was open for 25% of the time, Pallas kernels for 29%

commit v1 on v0

--- a/solution.py
+++ b/solution.py
@@ -152,7 +152,7 @@
 def front_kernel(cz_ref, ys_ref, slab_ref, t1_ref, l2_ref, q2_ref):
     depth, window_y, width = slab_ref.shape
     rows_y = 2 * BOX
-    chunk = 8
+    chunk = 16
     t1 = t1_ref[...]
     l2 = l2_ref[...]
 

time: 265 us -> 239 us (0.902)
  Pallas kernels: 75.6 us -> 50.5 us
    pallas_call x1, Pallas kernels: 75.6 us -> 50.5 us  [front(): pl.pallas_call(front_kernel, grid_spec=grid_spec, out_shape=jax.ShapeDtyp...]
  transfers between devices with their start and end apart: 1 -> 1, of which waited for: 0 -> 0; matrix products, arithmetic and copies ran while one was open for 25% -> 27% of each run, Pallas kernels for 29% -> 21%
where the time goes in v1:
time: 239 us; the launch traced here: 235 us
  matrix products  90.3 us (38%)
  other arithmetic  66 us (28%)
  Pallas kernels  50.5 us (21%)
  between operations  16.1 us (7%)
  local copies, waits for them, and re-layouts  12 us (5%)
    pallas_call x1, Pallas kernels, front(): pl.pallas_call(front_kernel, grid_spec=grid_spec, out_shape=jax.ShapeDtyp...  50.5 us
    dot_general x12, matrix products, section(): jnp.einsum(pattern, bf(operand), table, preferred_element_type=jnp.float32)  45.1 us
    another operation x2, other arithmetic, one(): cross = jnp.stack([bf(real_p), bf(imag_p)], axis=2)  38.6 us
    dot_general x1, matrix products, box_spectra_of(): jnp.einsum('nwzkq,wzh->nhkq', q2, l3, preferred_element_type=jnp.float32)  32.2 us
    dot_general x1, matrix products, block_rms(): sums_y = jnp.einsum('zynu,nty->nztu', sums_x, band_y, precision=hi)  5.05 us
  transfers between devices with their start and end apart: 1, of which 0 were waited for; matrix products, arithmetic and copies ran while one was open for 27% of the time, Pallas kernels for 21%

profile of v1, /device:TPU:0, one launch (start us, length us, event | category | flops | bytes accessed | tf_op | source)
XLA Modules:
  0.0 235.0 jit_solution(8670514500886118974)
XLA Ops:
  7.5 1.5 convert_reduce_fusion
  9.6 1.5 fusion.144
  11.8 0.9 fusion.145
  13.8 0.5 reshape.1177
  14.2 0.4 convolution_convert_fusion
  14.6 0.3 copy.53
  15.5 0.4 copy_negate_fusion
  16.2 0.4 fusion.69
  16.6 1.0 copy.54
  17.9 0.6 reduce_sum.27
  18.5 0.6 iota_compare_fusion.8
  19.6 4.4 %fusion.135 = (bf16[15,256,1,64]{1,3,2,0:T(8,128)(2,1)S(1)}, bf16[15,256,1,64]{1,3,2,0:T(8,128)(2,1)S(1)}) fusion(s32[15,256]{1,0:T(8,128)S(1)} %iota_subtract_fusion, pred[15,256]{1,0:T(8,128)(4,1)S(1)} %compare_and_fusion), kind=kLoop, calls=%fused_computation.159 | loop fusion | flops 5160960 | bytes 1002240 | tf_op jit(solution)/shard_map/jit(_where)/select_n | solution.py:94
  24.1 0.8 copy.56.t1_ref
  24.9 4.2 %convert_multiply_fusion.16 = f32[80,128,256]{2,1,0:T(8,128)S(1)} fusion(bf16[80,128,256]{2,1,0:T(8,128)(2,1)} %slab_ref.1), kind=kLoop, calls=%fused_computation.55 | loop fusion | flops 5242880 | bytes 15728640 | tf_op jit(solution)/shard_map/mul | solution.py:192
  29.2 1.4 fusion.30
  30.7 1.8 fusion.147
  32.5 1.8 fusion.68
  34.3 5.1 %fusion.106 = f32[15,80,8,8]{1,2,3,0:T(8,128)S(1)} fusion(f32[80,128,15,8]{1,3,0,2:T(8,128)S(1)} %fusion.68, s32[15,8]{1,0:T(8,128)S(1)} %get-tuple-element.47, s32[15,8]{1,0:T(8,128)S(1)} %get-tuple-element.48), kind=kOutput, calls=%fused_computation.109 | convolution fusion | flops 118010880 | bytes 5223360 | tf_op jit(solution)/shard_map/zynu,nty->nztu/dot_general | solution.py:200
  39.4 3.4 %fusion.140 = f32[15,8,8,8]{3,1,2,0:T(8,128)S(1)} fusion(f32[15,80,8,8]{1,2,3,0:T(8,128)S(1)} %fusion.106, s32[15,8]{1,0:T(8,128)S(1)} %get-tuple-element.42, s32[15,8]{1,0:T(8,128)S(1)} %get-tuple-element.41), kind=kOutput, calls=%fused_computation.164 | convolution fusion | flops 7401600 | bytes 338880 | tf_op jit(solution)/shard_map/nztu,nsz->nstu/dot_general | solution.py:202
  42.8 0.5 copy.64
  43.3 4.8 %fusion.148 = (bf16[15,128,64]{2,1,0:T(8,128)(2,1)S(1)}, bf16[15,128,64]{2,1,0:T(8,128)(2,1)S(1)}, bf16[15,128,64]{2,1,0:T(8,128)(2,1)S(1)}) fusion(s32[15,128]{1,0:T(8,128)S(1)} %iota_subtract_fusion.1, pred[15,128]{1,0:T(8,128)(4,1)S(1)} %compare_and_fusion.1), kind=kLoop, calls=%fused_computation.178 | loop fusion | flops 2580480 | bytes 746880 | tf_op jit(solution)/shard_map/neg | solution.py:223
  48.1 0.5 maximum_maximum_fusion.l2_ref
  48.6 50.5 %shard_map.77 = bf16[15,2,64,64,128]{4,3,2,1,0:T(8,128)(2,1)} custom-call(s32[15]{0:T(128)S(1)} %bitcast.325, s32[15]{0:T(128)S(1)} %get-tuple-element.7.ys_ref, bf16[80,128,256]{2,1,0:T(8,128)(2,1)} %slab_ref.1, bf16[15,256,128]{2,1,0:T(8,128)(2,1)S(1)} %copy.56.t1_ref, bf16[15,256,128]{2,1,0:T(8,128)(2,1)S(1)} %maximum_maximum_fusion.l2_ref), custom_call_target="tpu_custom_call" | custom-call | tf_op jit(solution)/shard_map/pallas_call | solution.py:238
  99.8 32.2 %fusion.31 = bf16[15,33,64,128]{3,1,2,0:T(8,128)(2,1)} fusion(bf16[15,2,64,64,128]{4,3,2,1,0:T(8,128)(2,1)} %shard_map.77, bf16[1,64,33]{1,2,0:T(8,128)(2,1)S(1)} %get-tuple-element.55, bf16[1,64,33]{1,2,0:T(8,128)(2,1)S(1)} %get-tuple-element.56), kind=kOutput, calls=%fused_computation.56 | convolution fusion | flops 1042162176 | bytes 39575808 | tf_op jit(solution)/shard_map/nwzkq,wzh->nhkq/dot_general | solution.py:250
  132.1 3.6 %slice_convert_fusion.7 = (f32[33,64,64]{2,1,0:T(8,128)S(1)}, f32[33,64,64]{2,1,0:T(8,128)S(1)}, f32[33,64,64]{2,1,0:T(8,128)S(1)}, f32[33,64,64]{2,1,0:T(8,128)...) fusion(bf16[132,64,128]{2,1,0:T(8,128)(2,1)} %all-gather.3.clon, ...), kind=kLoop, calls=%fused_computation.151 | loop fusion | flops 1081344 | bytes 6488064 | tf_op jit(solution)/shard_map/convert_element_type | solution.py:259
  135.7 0.6 copy.55
  136.3 0.6 copy.76
  137.0 0.6 copy.71
  137.7 0.6 copy.70
  138.3 0.6 copy.66
  138.9 0.6 copy.65
  139.6 1.7 copy.58
  141.3 1.7 copy.75
  143.0 11.0 %fusion.37 = (bf16[15,1,1,33,64,64]{5,3,4,0,2,1:T(8,128)(2,1)}, bf16[15,1,1,33,64,64]{5,3,4,0,2,1:T(8,128)(2,1)}) fusion(f32[33,64,64]{2,0,1:T(8,128)S(1)} %copy.66, f32[33,64,64]{2,0,1:T(8,128)S(1)} %copy.65, bf16[15,33,64,128]{3,1,2,0:T(8,128)(2,1)S(1)} %bitcast.327), kind=kLoop, calls=%fused_computation.62 | loop fusion | flops 20275200 | bytes 17301504 | tf_op jit(solution)/shard_map/stack | solution.py:265
  154.1 9.9 %fusion.45 = bf16[15,2,8,64,64]{4,2,3,0,1:T(8,128)(2,1)} fusion(bf16[1,33,2,8]{1,3,0,2:T(8,128)(2,1)S(1)} %get-tuple-element.40, bf16[1,33,2,8]{1,3,0,2:T(8,128)(2,1)S(1)} %get-tuple-element.39, bf16[15,1,1,33,64,64]{5,3,4,0,2,1:T(8,128)(2,1)} %get-tuple-element.11, bf16[15,1,1,33,64,64]{5,3,4,0,2,1:T(8,128)(2,1)} %get-tuple-element.10), kind=kOutput, calls=%fused_computation.72 | convolution fusion | flops 134803584 | bytes 10078272 | tf_op jit(solution)/shard_map/nrchkj,chds->nrdskj/dot_general | solution.py:48
  164.0 27.6 %fusion.39 = (bf16[15,1,1,33,64,64]{5,3,4,0,2,1:T(8,128)(2,1)}, bf16[15,1,1,33,64,64]{5,3,4,0,2,1:T(8,128)(2,1)}, bf16[15,1,1,33,64,64]{5,3,4,0,2,1:T(8,128)(2,1...) fusion(f32[33,64,64]{2,0,1:T(8,128)} %copy.58, ...), kind=kLoop, calls=%fused_computation.64 | loop fusion | flops 52715520 | bytes 35684352 | tf_op jit(solution)/shard_map/stack | solution.py:265
  191.5 8.8 %fusion.44 = bf16[15,2,8,64,64]{4,2,3,0,1:T(8,128)(2,1)S(1)} fusion(bf16[1,33,2,8]{1,3,0,2:T(8,128)(2,1)S(1)} %get-tuple-element.40, bf16[1,33,2,8]{1,3,0,2:T(8,128)(2,1)S(1)} %get-tuple-element.39, bf16[15,1,1,33,64,64]{5,3,4,0,2,1:T(8,128)(2,1)} %get-tuple-element.9, bf16[15,1,1,33,64,64]{5,3,4,0,2,1:T(8,128)(2,1)} %get-tuple-element.8), kind=kOutput, calls=%fused_computation.71 | convolution fusion | flops 134803584 | bytes 10078272 | tf_op jit(solution)/shard_map/nrchkj,chds->nrdskj/dot_general | solution.py:48
  200.3 1.6 fusion.97
  201.9 1.6 fusion.94
  203.6 0.8 fusion.112
  204.4 0.8 fusion.110
  205.1 9.0 %fusion.46 = bf16[15,2,8,64,64]{4,2,3,0,1:T(8,128)(2,1)S(1)} fusion(bf16[1,33,2,8]{1,3,0,2:T(8,128)(2,1)S(1)} %get-tuple-element.40, bf16[1,33,2,8]{1,3,0,2:T(8,128)(2,1)S(1)} %get-tuple-element.39, bf16[15,1,1,33,64,64]{5,3,4,0,2,1:T(8,128)(2,1)} %get-tuple-element.18, bf16[15,1,1,33,64,64]{5,3,4,0,2,1:T(8,128)(2,1)} %get-tuple-element.19), kind=kOutput, calls=%fused_computation.73 | convolution fusion | flops 134803584 | bytes 10078272 | tf_op jit(solution)/shard_map/nrchkj,chds->nrdskj/dot_general | solution.py:48
  214.1 1.6 fusion.100
  215.8 7.8 %fusion.47 = bf16[15,2,8,64,64]{4,2,3,0,1:T(8,128)(2,1)S(1)} fusion(bf16[1,33,2,8]{1,3,0,2:T(8,128)(2,1)S(1)} %get-tuple-element.40, bf16[1,33,2,8]{1,3,0,2:T(8,128)(2,1)S(1)} %get-tuple-element.39, bf16[15,1,1,33,64,64]{5,3,4,0,2,1:T(8,128)(2,1)S(1)} %bitcast.329, bf16[15,1,1,33,64,64]{5,3,4,0,2,1:T(8,128)(2,1)} %get-tuple-element.17), kind=kOutput, calls=%fused_computation.74 | convolution fusion | flops 134803584 | bytes 10078272 | tf_op jit(solution)/shard_map/nrchkj,chds->nrdskj/dot_general | solution.py:48
  223.6 1.6 fusion.103
  225.3 0.8 fusion.116
  226.0 0.8 fusion.114
  226.8 1.1 fusion.220
  (60 shorter events, 3.9 us)
Async XLA Ops:
  7.2 10.4 %copy-start.3 = (s32[1,15]{1,0:T(1,128)S(1)}, s32[1,15]{1,0:T(1,128)}, u32[]{:S(2)}) copy-start(s32[1,15]{1,0:T(1,128)} %param.9) | copy-start | bytes 184
  7.2 10.6 %copy-start.2 = (s32[1,15]{1,0:T(1,128)S(1)}, s32[1,15]{1,0:T(1,128)}, u32[]{:S(2)}) copy-start(s32[1,15]{1,0:T(1,128)} %param.10) | copy-start | bytes 184
  7.2 10.7 %copy-start.4 = (s32[1,1,8]{2,1,0:T(1,128)S(1)}, s32[1,1,8]{2,1,0:T(1,128)}, u32[]{:S(2)}) copy-start(s32[1,1,8]{2,1,0:T(1,128)} %param.11) | copy-start | bytes 100
  7.2 124.9 %all-gather.3.cloned.1.call-start = ((), (), s32[]{:S(2)}) async-start(), calls=%async_computation | async-start | bytes 2703360 | tf_op jit(solution)/shard_map/all_gather | solution.py:300
  29.1 1.5 copy-start
  132.1 10.9 %slice-start = ((s8[9830400]{0:T(1024)(128)(4,1)}), s8[4194304]{0:T(1024)(128)(4,1)S(1)}, s32[]{:S(2)}) async-start(s8[9830400]{0:T(1024)(128)(4,1)} %bitcast.326), calls=%async_computation.1 | async-start | bytes 8388608
  132.1 10.9 %slice-start.1 = ((s8[9830400]{0:T(1024)(128)(4,1)}), s8[4194304]{0:T(1024)(128)(4,1)S(1)}, s32[]{:S(2)}) async-start(s8[9830400]{0:T(1024)(128)(4,1)} %bitcast.326), calls=%async_computation.2 | async-start | bytes 8388608
  137.6 5.4 %slice-start.2 = ((s8[9830400]{0:T(1024)(128)(4,1)}), s8[1441792]{0:T(1024)(128)(4,1)S(1)}, s32[]{:S(2)}) async-start(s8[9830400]{0:T(1024)(128)(4,1)} %bitcast.326), calls=%async_computation.3 | async-start | bytes 2883584
  191.5 8.8 %copy-start.1 = (bf16[15,2,8,64,64]{4,2,3,0,1:T(8,128)(2,1)S(1)}, bf16[15,2,8,64,64]{4,2,3,0,1:T(8,128)(2,1)}, u32[]{:S(2)}) copy-start(bf16[15,2,8,64,64]{4,2,3,0,1:T(8,128)(2,1)} %fusion.45) | copy-start | bytes 5898244
  204.3 11.4 %slice-start.3 = ((s8[9830400]{0:T(1024)(128)(4,1)}), s8[4194304]{0:T(1024)(128)(4,1)S(1)}, s32[]{:S(2)}) async-start(s8[9830400]{0:T(1024)(128)(4,1)} %bitcast.328), calls=%async_computation.4 | async-start | bytes 8388608
  205.1 10.6 %slice-start.4 = ((s8[9830400]{0:T(1024)(128)(4,1)}), s8[4194304]{0:T(1024)(128)(4,1)S(1)}, s32[]{:S(2)}) async-start(s8[9830400]{0:T(1024)(128)(4,1)} %bitcast.328), calls=%async_computation.5 | async-start | bytes 8388608
  205.1 10.7 %slice-start.5 = ((s8[9830400]{0:T(1024)(128)(4,1)}), s8[1441792]{0:T(1024)(128)(4,1)S(1)}, s32[]{:S(2)}) async-start(s8[9830400]{0:T(1024)(128)(4,1)} %bitcast.328), calls=%async_computation.6 | async-start | bytes 2883584
Sparse Core Ops, SparseCore 0:
  17.7 25.6 all-gather.2
